TPU v7x, 128 devices: a whole 4x4x4 slice. The times are simulated.
128 devices in a mesh: grp: 4 (over x), gx: 4 (over y), gy: 8 (over z, core).
Axes of the slice: x: 4, y: 4, z: 4, core: 2. Of those that a mesh axis runs over, the one named last changes fastest.
Arguments:
- modes_now: float32 [4, 32, 512, 1024], P('grp', ('gx', 'gy')), may hold values from -6 to 6
- modes_old: float32 [4, 32, 512, 1024], P('grp', ('gx', 'gy')), may hold values from -6 to 6
- pressure_now: float32 [4, 32, 512, 1024], P('grp', None, 'gx', 'gy'), may hold values from -6 to 6
- source: float32 [4, 32, 512, 1024], P('grp', None, 'gx', 'gy'), may hold values from -6 to 6
- strip_slot: int32 [4, 512, 8], P('grp', 'gx', 'gy'), may hold values from 0 to 255, as said below
- strip_row: int32 [4, 512, 8], P('grp', 'gx', 'gy'), may hold values from 0 to 127, as said below
Outputs:
- modes_new: float32 [4, 32, 512, 1024], P('grp', ('gx', 'gy'))
- pressure_next: float32 [4, 32, 512, 1024], P('grp', None, 'gx', 'gy')
Inputs may be any that keep to these rules, and one draw needn't show every extreme that they name: The 128 strips of one device take distinct values of strip_slot. Each device sends to every other device (itself included) either no strip or exactly 2, and every bottom-face strip of every device is met by exactly one top-face strip. `strip_row`: see strip_slot.
All inputs are finite; a program needn't handle non-finite values.
Results may differ from a plain program's by a relative error of at most 0.00007.
Values sent between devices are 32-bit elements; how exact they have to be, the bound alone decides.
No kernel may reach another device: no remote copies, remote signals or barrier semaphores. Data moves between devices by JAX's collectives and lax.ppermute only.
A program may use at most 64 MiB of HBM per device.

v0:
```python
import jax
import jax.numpy as jnp
from jax import lax
from jax.sharding import PartitionSpec as P

COURANT = 0.5
WEIGHTS = (1.5, -0.15, 2.0 / 180.0)
HIGH = lax.Precision.HIGHEST
FAST = lax.Precision.HIGH


def cosine_table(count):
    rows = jnp.arange(count, dtype=jnp.int32).astype(jnp.float32)[:, None]
    cols = jnp.arange(count, dtype=jnp.int32).astype(jnp.float32)[None, :]
    scale = jnp.where(rows == 0, jnp.sqrt(1.0 / count), jnp.sqrt(2.0 / count))
    return scale * jnp.cos(jnp.pi * rows * (cols + 0.5) / count)


def face_stencil(diff):
    first = diff[..., 0, :]
    second = diff[..., 1, :]
    third = diff[..., 2, :]
    return jnp.stack(
        [
            WEIGHTS[0] * first + WEIGHTS[1] * second + WEIGHTS[2] * third,
            WEIGHTS[1] * first + WEIGHTS[2] * second,
            WEIGHTS[2] * first,
        ],
        axis=-2,
    )


def to_modes(field, table_z, table_x, table_y):
    width_x = lax.axis_size("gx")
    width_y = lax.axis_size("gy")
    rows_x = field.shape[2]
    cols_y = field.shape[3]
    part = jnp.einsum("kz,zxy->kxy", table_z, field[0], precision=HIGH)
    part = lax.all_to_all(part, ("gx", "gy"), split_axis=0, concat_axis=0, tiled=True)
    part = part.reshape(width_x, width_y, rows_x, cols_y)
    split_x = table_x.reshape(table_x.shape[0], width_x, rows_x)
    split_y = table_y.reshape(table_y.shape[0], width_y, cols_y)
    part = jnp.einsum("bix,ijxy->bjy", split_x, part, precision=FAST)
    return jnp.einsum("cjy,bjy->bc", split_y, part, precision=FAST)[None, None]


def to_cells(modes, table_z, table_x, table_y):
    width_x = lax.axis_size("gx")
    width_y = lax.axis_size("gy")
    rows_x = modes.shape[2] // width_x
    cols_y = modes.shape[3] // width_y
    split_x = table_x.reshape(table_x.shape[0], width_x, rows_x)
    split_y = table_y.reshape(table_y.shape[0], width_y, cols_y)
    part = jnp.einsum("cjy,bc->bjy", split_y, modes[0, 0], precision=FAST)
    part = jnp.einsum("bix,bjy->ijxy", split_x, part, precision=FAST)
    part = part.reshape(width_x * width_y, rows_x, cols_y)
    cells = lax.all_to_all(part, ("gx", "gy"), split_axis=0, concat_axis=0, tiled=True)
    return jnp.einsum("kz,kxy->zxy", table_z, cells, precision=HIGH)[None]


def advance_terms(depth_index, depth, long_x, long_y):
    index_x = jnp.arange(long_x, dtype=jnp.int32).astype(jnp.float32)
    index_y = jnp.arange(long_y, dtype=jnp.int32).astype(jnp.float32)
    part_z = depth_index / depth * (depth_index / depth)
    part_x = index_x / long_x * (index_x / long_x)
    part_y = index_y / long_y * (index_y / long_y)
    theta = (
        COURANT
        * jnp.pi
        * jnp.sqrt(part_z[:, None, None] + part_x[None, :, None] + part_y[None, None, :])
    )
    shape = jnp.sinc(theta / (2.0 * jnp.pi))
    return (2.0 * jnp.cos(theta), COURANT * COURANT * shape * shape)


def lane_stencil(diff, cols):
    first = diff[:, :cols]
    second = diff[:, cols : 2 * cols]
    third = diff[:, 2 * cols :]
    return jnp.concatenate(
        [
            WEIGHTS[0] * first + WEIGHTS[1] * second + WEIGHTS[2] * third,
            WEIGHTS[1] * first + WEIGHTS[2] * second,
            WEIGHTS[2] * first,
        ],
        axis=1,
    )


def one_hot(index, count):
    return (index[:, None] == jnp.arange(count, dtype=jnp.int32)[None, :]).astype(jnp.float32)


def shards(modes_now, modes_old, pressure_now, source, strip_slot, strip_row):
    depth = source.shape[1]
    rows_x = source.shape[2]
    cols_y = source.shape[3]
    planes = modes_now.shape[1]
    long_x = modes_now.shape[2]
    long_y = modes_now.shape[3]
    block = lax.axis_index(("gx", "gy"))
    depth_index = (block * planes + jnp.arange(planes, dtype=jnp.int32)).astype(jnp.float32)
    table_z = lax.optimization_barrier(cosine_table(depth))
    table_x = lax.optimization_barrier(cosine_table(long_x))
    table_y = lax.optimization_barrier(cosine_table(long_y))
    scale_now, scale_spec = advance_terms(depth_index, depth, long_x, long_y)
    scale_now = lax.optimization_barrier(scale_now)
    scale_spec = lax.optimization_barrier(scale_spec)
    top = jnp.stack(
        [pressure_now[0, depth - 1], pressure_now[0, depth - 2], pressure_now[0, depth - 3]], axis=1
    ).reshape(rows_x, 3 * cols_y)
    bottom = jnp.transpose(pressure_now[0, 0:3], (1, 0, 2)).reshape(rows_x, 3 * cols_y)
    every = ("grp", "gx", "gy")
    devices = lax.axis_size(every)
    slots_per = max(2, rows_x // devices)
    total = devices * slots_per
    slots = strip_slot.reshape(-1)
    mine = (slots * rows_x + strip_row.reshape(-1)).astype(jnp.float32)
    owner = jnp.arange(devices, dtype=jnp.int32)[:, None] == lax.axis_index(every)
    codes = lax.psum(jnp.where(owner, mine[None, :], 0.0), every)
    codes = jnp.round(codes).astype(jnp.int32)
    want = lax.axis_index(every) * slots_per + jnp.arange(slots_per, dtype=jnp.int32)
    hit = (codes // rows_x)[:, :, None] == want[None, None, :]
    found = jnp.any(hit, axis=1).reshape(total)
    marks = jnp.sum(jnp.where(hit, (codes % rows_x)[:, :, None], 0), axis=1).reshape(total)
    marks = jnp.where(found, marks, -1)
    send = one_hot(slots, total)
    meet = one_hot(marks, rows_x)
    rims_out = jnp.einsum("sk,sf->kf", send, top, precision=HIGH)
    met = jnp.einsum("kr,rf->kf", meet, bottom, precision=HIGH)
    got = lax.all_to_all(
        jnp.concatenate([rims_out, met], axis=1), every, split_axis=0, concat_axis=0, tiled=True
    )
    rims = got[:, : 3 * cols_y]
    far = got[:, 3 * cols_y :]
    live = found.astype(jnp.float32)[:, None]
    force = lane_stencil(met - rims, cols_y) * live
    bottom_force = jnp.einsum("kr,kf->rf", meet, -force, precision=HIGH).reshape(rows_x, 3, cols_y)
    partner = jnp.einsum("sk,kf->sf", send, far, precision=HIGH)
    top_force = lane_stencil(partner - top, cols_y).reshape(rows_x, 3, cols_y)
    forcing = source.at[:, 0:3].add(jnp.transpose(bottom_force, (1, 0, 2))[None])
    forcing = forcing.at[:, depth - 1].add(top_force[:, 0][None])
    forcing = forcing.at[:, depth - 2].add(top_force[:, 1][None])
    forcing = forcing.at[:, depth - 3].add(top_force[:, 2][None])
    spectrum = to_modes(forcing, table_z, table_x, table_y)
    modes_new = (scale_now * modes_now[0] - modes_old[0] + scale_spec * spectrum[0])[None]
    pressure_next = to_cells(modes_new, table_z, table_x, table_y)
    return (modes_new, pressure_next)


def solution(mesh):
    placed = (
        P("grp", ("gx", "gy"), None, None),
        P("grp", ("gx", "gy"), None, None),
        P("grp", None, "gx", "gy"),
        P("grp", None, "gx", "gy"),
        P("grp", "gx", "gy"),
        P("grp", "gx", "gy"),
    )
    return jax.shard_map(
        shards,
        mesh=mesh,
        in_specs=placed,
        out_specs=(P("grp", ("gx", "gy"), None, None), P("grp", None, "gx", "gy")),
        check_vma=False,
    )
```

profile of v0, /device:TPU:1, one launch (start us, length us, event | category | flops | bytes accessed | tf_op | source)
XLA Modules:
  0.0 294.6 jit_solution(2548714859366596820)
XLA Ops:
  7.2 0.0 slice-start
  7.2 0.0 all-reduce.2.cloned.1.call-start
  7.2 0.7 fusion.64
  8.0 0.7 broadcast_select_fusion
  8.7 0.0 all-reduce.2.cloned.1.call-update
  8.7 0.9 fusion.66
  9.6 0.1 copy.109
  9.7 0.1 copy.110
  9.8 0.1 copy.111
  9.9 1.1 fusion.43
  11.0 0.0 slice-done
  11.1 0.1 copy.108
  11.2 145.1 %all-reduce.2.cloned.1.call-done = f32[128,128]{1,0:T(8,128)} async-done(((f32[128,128]{1,0:T(8,128)}), f32[128,128]{1,0:T(8,128)}) %all-reduce.2.cloned.1.call-update) | async-done | bytes 65552 | tf_op jit(solution)/shard_map/psum | solution.py:120
  156.3 0.9 add_select_fusion
  157.2 0.2 compare_reduce_fusion
  157.4 0.2 fusion.39
  157.6 0.1 copy.74
  157.7 0.1 select_n.132
  157.8 0.0 copy-start.2
  157.8 0.5 copy-done.2
  158.4 0.4 fusion.42
  158.7 0.1 pad_maximum_fusion
  158.8 1.3 all_to_all.14
  160.1 5.1 %all-to-all-start = ((f32[128,2,768]{2,1,0:T(2,128)}), f32[128,2,768]{2,1,0:T(2,128)S(1)}, u32[]{:S(2)}, u32[]{:S(2)}) async-start(f32[128,2,768]{2,1,0:T(2,128)} %all_to_all.14), calls=%async_computation | async-start | bytes 1572864 | tf_op jit(solution)/shard_map/all_to_all | solution.py:131
  165.2 0.1 copy.82
  165.4 0.1 cosine_multiply_fusion.3
  165.5 1.9 copy.81
  167.5 0.6 convert_element_type.98
  168.0 0.8 copy.79
  168.8 0.7 reshape.563
  169.5 0.0 copy-start.4
  169.5 12.1 %all-to-all-done = f32[128,2,768]{2,1,0:T(2,128)S(1)} async-done(((f32[128,2,768]{2,1,0:T(2,128)}), f32[128,2,768]{2,1,0:T(2,128)S(1)}, u32[]{:S(2)}, u32[]{:S(2)}) %all-to-all-start) | async-done | bytes 786464 | tf_op jit(solution)/shard_map/all_to_all | solution.py:131
  181.6 1.4 all_to_all.16
  183.0 0.0 copy-start.3
  183.1 1.1 slice_subtract_fusion
  184.1 0.0 copy-done.4
  184.1 1.3 convolution_subtract_fusion
  185.5 0.1 fusion.40
  185.6 0.1 copy.83
  185.7 0.0 copy-done.3
  185.7 0.0 copy-done.5
  185.7 0.6 fusion.31
  186.3 0.1 fusion.37
  186.4 1.3 copy.120
  187.7 0.6 fusion.47
  188.4 2.4 copy.85
  190.8 1.9 fusion.60
  192.7 2.6 copy.86
  195.2 4.9 %all-to-all-start.1 = ((f32[32,128,128]{2,1,0:T(8,128)}), f32[32,128,128]{2,1,0:T(8,128)S(1)}, u32[]{:S(2)}, u32[]{:S(2)}) async-start(f32[32,128,128]{2,1,0:T(8,128)} %copy.86), calls=%async_computation.1 | async-start | bytes 4194304 | tf_op jit(solution)/shard_map/all_to_all | solution.py:39
  200.2 3.5 %cosine_multiply_fusion.2 = f32[512,512]{0,1:T(8,128)S(1)} fusion(f32[512]{0:T(512)S(1)} %get-tuple-element.75, f32[512]{0:T(512)S(1)} %get-tuple-element.76, f32[512]{0:T(512)S(1)} %fusion.63), kind=kLoop, calls=%fused_computation.42 | loop fusion | flops 786432 | bytes 1054720 | tf_op jit(solution)/shard_map/mul | solution.py:16
  203.7 15.1 %cosine_multiply_fusion = f32[1024,1024]{0,1:T(8,128)} fusion(f32[1024]{0:T(1024)S(1)} %get-tuple-element.73, f32[1024]{0:T(1024)S(1)} %get-tuple-element.74, f32[1024]{0:T(1024)S(1)} %fusion.62), kind=kLoop, calls=%fused_computation | loop fusion | flops 3145728 | bytes 4206592 | tf_op jit(solution)/shard_map/mul | solution.py:16
  218.8 11.3 %cosine_multiply_fusion.1 = (f32[1,512,1024]{2,1,0:T(8,128)}, f32[1,512,1024]{2,1,0:T(8,128)}) fusion(f32[1024]{0:T(1024)S(1)} %multiply_multiply_fusion.5, f32[512]{0:T(512)S(1)} %multiply_add_fusion.3), kind=kLoop, calls=%fused_computation.37 | loop fusion | flops 20447232 | bytes 4200448 | tf_op jit(solution)/shard_map/mul | solution.py:73
  230.1 0.0 all-to-all-done.1
  230.1 1.9 fusion.67
  232.1 0.3 copy-done
  232.3 7.0 %fusion.13 = f32[1,512,1024]{2,1,0:T(8,128)S(1)} fusion(f32[1,512,1024]{2,1,0:T(8,128)} %get-tuple-element.72, f32[1,1,512,1024]{3,2,1,0:T(8,128)} %param.15, f32[1,512,1024]{2,1,0:T(8,128)} %get-tuple-element.71, f32[1,1,512,1024]{3,2,1,0:T(8,128)} %param.14, f32[1024,8,128]{0,2,1:T(8,128)S(1)} %bitcast.106, f32[512,8,128,1]{2,0,1,3:T(8,128)S(1)} %fusion.67), kind=kOutput, calls=%fused_computation.22 | convolution fusion | flops 3223322624 | bytes 16777216 | tf_op jit(solution)/shard_map/cjy,bjy->bc/dot_general | solution.py:44
  239.4 0.0 copy-start.1
  239.4 3.5 %fusion.11 = f32[512,8,128]{0,2,1:T(8,128)S(1)} fusion(f32[1024,8,128]{0,2,1:T(8,128)S(1)} %bitcast.107, f32[1,512,1024]{2,1,0:T(8,128)S(1)} %fusion.13), kind=kOutput, calls=%fused_computation.19 | convolution fusion | flops 3221225472 | bytes 8388608 | tf_op jit(solution)/shard_map/cjy,bc->bjy/dot_general | solution.py:54
  242.9 0.0 copy-done.1
  242.9 1.8 fusion.24
  244.8 1.8 copy.93
  246.6 35.6 %all_to_all.22 = f32[32,128,128]{2,1,0:T(8,128)S(1)} all-to-all(f32[32,128,128]{2,1,0:T(8,128)} %bitcast.112), channel_id=1, replica_groups=mesh['grp'=4,'gx'=4,'gy'=8] {'gx','gy'}, dimensions={0} | all-to-all | bytes 4194304 | tf_op jit(solution)/shard_map/all_to_all | solution.py:57
  282.2 3.0 %fusion.21 = f32[1,32,128,128]{3,1,2,0:T(8,128)S(1)} fusion(f32[32,128,128]{2,1,0:T(8,128)S(1)} %all_to_all.22, f32[32,32]{0,1:T(8,128)S(1)} %cosine_multiply_fusion.3), kind=kOutput, calls=%fused_computation.39 | convolution fusion | flops 201326592 | bytes 4198400 | tf_op jit(solution)/shard_map/kz,kxy->zxy/dot_general | solution.py:58
  285.2 2.5 copy.95
  (18 shorter events, 0.1 us)
Async XLA Ops:
  7.2 3.9 %slice-start = ((f32[1,32,128,128]{3,2,1,0:T(8,128)}), f32[1,3,128,128]{3,2,1,0:T(8,128)S(1)}, s32[]{:S(2)}) async-start(f32[1,32,128,128]{3,2,1,0:T(8,128)} %param.16), calls=%async_computation.4 | async-start | bytes 393216 | tf_op jit(solution)/shard_map/slice | solution.py:112
  7.2 149.1 %all-reduce.2.cloned.1.call-start = ((), (), s32[]{:S(2)}) async-start(), calls=%async_computation.3 | async-start | bytes 131072 | tf_op jit(solution)/shard_map/psum | solution.py:120
  157.8 0.5 copy-start.2
  160.1 21.5 %all-to-all-start = ((f32[128,2,768]{2,1,0:T(2,128)}), f32[128,2,768]{2,1,0:T(2,128)S(1)}, u32[]{:S(2)}, u32[]{:S(2)}) async-start(f32[128,2,768]{2,1,0:T(2,128)} %all_to_all.14), calls=%async_computation | async-start | bytes 1572864 | tf_op jit(solution)/shard_map/all_to_all | solution.py:131
  169.5 14.6 %copy-start.4 = (s32[1,128,1]{1,2,0:T(1,128)S(1)}, s32[1,128,1]{1,2,0:T(1,128)}, u32[]{:S(2)}) copy-start(s32[1,128,1]{1,2,0:T(1,128)} %param.18) | copy-start | bytes 1540
  183.0 2.7 copy-start.3
  183.1 2.7 copy-start.5
  195.2 34.9 %all-to-all-start.1 = ((f32[32,128,128]{2,1,0:T(8,128)}), f32[32,128,128]{2,1,0:T(8,128)S(1)}, u32[]{:S(2)}, u32[]{:S(2)}) async-start(f32[32,128,128]{2,1,0:T(8,128)} %copy.86), calls=%async_computation.1 | async-start | bytes 4194304 | tf_op jit(solution)/shard_map/all_to_all | solution.py:39
  230.1 2.2 copy-start
  239.4 3.6 %copy-start.1 = (f32[1,512,1024]{2,1,0:T(8,128)}, f32[1,512,1024]{2,1,0:T(8,128)S(1)}, u32[]{:S(2)}) copy-start(f32[1,512,1024]{2,1,0:T(8,128)S(1)} %fusion.13) | copy-start | bytes 6291460
Sparse Core Ops, SparseCore 0:
  13.3 142.9 all-reduce.1
where the time goes:
time: 295 us
  waiting for transfers between devices  157 us (53%)
  blocking collectives  35.6 us (12%)
  other arithmetic  35.3 us (12%)
  matrix products  22.6 us (8%)
  local copies, waits for them, and re-layouts  19.4 us (7%)
  between operations  14.4 us (5%)
  starting transfers between devices  10 us (3%)
    psum x1, waiting for transfers between devices, shards(): codes = lax.psum(jnp.where(owner, mine[None, :], 0.0), every)  145 us
    all_to_all x1, blocking collectives, to_cells(): lax.all_to_all(part, ('gx', 'gy'), split_axis=0, concat_axis=0, tiled=True)  35.6 us
    mul x4, other arithmetic, cosine_table(): return scale * jnp.cos(jnp.pi * rows * (cols + 0.5) / count)  18.7 us
    all_to_all x1, waiting for transfers between devices, shards(): lax.all_to_all(jnp.concatenate([rims_out, met], axis=1), every, split_axi...  12.1 us
    mul x1, other arithmetic, advance_terms(): return (2.0 * jnp.cos(theta), COURANT * COURANT * shape * shape)  11.3 us
    dot_general x1, matrix products, to_modes(): return jnp.einsum('cjy,bjy->bc', split_y, part, precision=FAST)[None, None]  7.03 us
    unnamed x19, local copies, waits for them, and re-layouts  7.02 us
  transfers between devices with their start and end apart: 3, of which 2 were waited for; matrix products, arithmetic and copies ran while one was open for 12% of the time, Pallas kernels for 0%

commit v1 on v0

--- a/solution.py
+++ b/solution.py
@@ -117,7 +117,7 @@
     slots = strip_slot.reshape(-1)
     mine = (slots * rows_x + strip_row.reshape(-1)).astype(jnp.float32)
     owner = jnp.arange(devices, dtype=jnp.int32)[:, None] == lax.axis_index(every)
-    codes = lax.psum(jnp.where(owner, mine[None, :], 0.0), every)
+    codes = jnp.sum(lax.all_gather(jnp.where(owner, mine[None, :], 0.0), every), axis=0)
     codes = jnp.round(codes).astype(jnp.int32)
     want = lax.axis_index(every) * slots_per + jnp.arange(slots_per, dtype=jnp.int32)
     hit = (codes // rows_x)[:, :, None] == want[None, None, :]

time: 295 us -> 227 us (0.77)
  waiting for transfers between devices: 157 us -> 85.5 us
  other arithmetic: 35.3 us -> 38.3 us
    psum x1 -> x0, waiting for transfers between devices: 145 us -> none  [shards(): codes = lax.psum(jnp.where(owner, mine[None, :], 0.0), every)]
    all_gather x0 -> x1, waiting for transfers between devices: none -> 73.4 us  [shards(): lax.all_gather(jnp.where(owner, mine[None, :], 0.0), every)]
    reduce_sum x0 -> x1, other arithmetic: none -> 3.81 us  [shards(): jnp.sum(lax.all_gather(jnp.where(owner, mine[None, :], 0.0), every), axis=0)]
    unnamed x19 -> x21, local copies, waits for them, and re-layouts: 7.02 us -> 7.02 us
  transfers between devices with their start and end apart: 3 -> 3, of which waited for: 2 -> 2; matrix products, arithmetic and copies ran while one was open for 12% -> 16% of each run, Pallas kernels for 0% -> 0%
where the time goes in v1:
time: 227 us; the launch traced here: 226 us
  waiting for transfers between devices  85.5 us (38%)
  other arithmetic  38.3 us (17%)
  blocking collectives  35.6 us (16%)
  matrix products  21.9 us (10%)
  local copies, waits for them, and re-layouts  20.4 us (9%)
  between operations  14.4 us (6%)
  starting transfers between devices  10.3 us (5%)
    all_gather x1, waiting for transfers between devices, shards(): lax.all_gather(jnp.where(owner, mine[None, :], 0.0), every)  73.4 us
    all_to_all x1, blocking collectives, to_cells(): lax.all_to_all(part, ('gx', 'gy'), split_axis=0, concat_axis=0, tiled=True)  35.6 us
    mul x4, other arithmetic, cosine_table(): return scale * jnp.cos(jnp.pi * rows * (cols + 0.5) / count)  18.7 us
    all_to_all x1, waiting for transfers between devices, shards(): lax.all_to_all(jnp.concatenate([rims_out, met], axis=1), every, split_axi...  12.1 us
    mul x1, other arithmetic, advance_terms(): return (2.0 * jnp.cos(theta), COURANT * COURANT * shape * shape)  11.3 us
    dot_general x1, matrix products, to_modes(): return jnp.einsum('cjy,bjy->bc', split_y, part, precision=FAST)[None, None]  7.03 us
    unnamed x21, local copies, waits for them, and re-layouts  7.02 us
    all_to_all x1, starting transfers between devices, shards(): lax.all_to_all(jnp.concatenate([rims_out, met], axis=1), every, split_axi...  5.35 us
  transfers between devices with their start and end apart: 3, of which 2 were waited for; matrix products, arithmetic and copies ran while one was open for 16% of the time, Pallas kernels for 0%

profile of v1, /device:TPU:1, one launch (start us, length us, event | category | flops | bytes accessed | tf_op | source)
XLA Modules:
  0.0 226.4 jit_solution(3146035619721594867)
XLA Ops:
  7.2 0.0 copy-start.4
  7.2 0.0 all-gather.2.cloned.1.call-start
  7.2 0.7 fusion.64
  7.9 0.7 broadcast_select_fusion
  8.6 0.0 all-gather.2.cloned.1.call-update
  8.7 0.9 slice.156
  9.6 0.1 copy.108
  9.7 0.9 fusion.66
  10.7 0.1 copy.109
  10.8 0.1 copy.110
  10.9 0.1 copy.111
  11.0 0.0 copy-done.4
  11.0 0.4 fusion.43
  11.4 73.4 %all-gather.2.cloned.1.call-done = f32[128,128,128]{2,1,0:T(8,128)} async-done(((f32[1,128,128]{2,1,0:T(8,128)}), f32[128,128,128]{2,1,0:T(8,128)}) %all-gather.2.cloned.1.call-update) | async-done | bytes 8388624 | tf_op jit(solution)/shard_map/all_gather | solution.py:120
  84.8 3.8 %reduce_sum.18 = f32[128,128]{1,0:T(8,128)S(1)} reduce(f32[128,128,128]{2,1,0:T(8,128)} %all-gather.2.cloned.1.call-done, f32[]{:T(128)} %constant.223.clone.1), dimensions={0}, to_apply=%region_0.1 | reduce | flops 2080768 | bytes 8454148 | tf_op jit(solution)/shard_map/reduce_sum | solution.py:120
  88.6 0.1 add_select_fusion
  88.7 0.2 compare_reduce_fusion
  88.9 0.2 fusion.39
  89.1 0.1 copy.74
  89.2 0.1 select_n.147
  89.3 0.0 copy-start.2
  89.3 0.5 copy-done.2
  89.9 0.4 fusion.42
  90.2 0.1 pad_maximum_fusion
  90.3 1.3 all_to_all.14
  91.6 5.4 %all-to-all-start = ((f32[128,2,768]{2,1,0:T(2,128)}), f32[128,2,768]{2,1,0:T(2,128)S(1)}, u32[]{:S(2)}, u32[]{:S(2)}) async-start(f32[128,2,768]{2,1,0:T(2,128)} %all_to_all.14), calls=%async_computation | async-start | bytes 1572864 | tf_op jit(solution)/shard_map/all_to_all | solution.py:131
  97.0 0.1 copy.82
  97.2 0.1 cosine_multiply_fusion.3
  97.3 1.9 copy.81
  99.2 0.6 convert_element_type.105
  99.8 0.8 copy.79
  100.6 0.7 reshape.636
  101.3 12.1 %all-to-all-done = f32[128,2,768]{2,1,0:T(2,128)S(1)} async-done(((f32[128,2,768]{2,1,0:T(2,128)}), f32[128,2,768]{2,1,0:T(2,128)S(1)}, u32[]{:S(2)}, u32[]{:S(2)}) %all-to-all-start) | async-done | bytes 786464 | tf_op jit(solution)/shard_map/all_to_all | solution.py:131
  113.4 1.4 all_to_all.16
  114.8 1.1 slice_subtract_fusion
  115.9 0.0 copy-done.5
  115.9 1.3 convolution_subtract_fusion
  117.2 0.1 fusion.40
  117.3 0.1 copy.83
  117.5 0.0 copy-done.3
  117.5 0.0 copy-done.6
  117.5 0.6 fusion.31
  118.1 0.1 fusion.37
  118.2 1.3 copy.119
  119.5 0.6 fusion.47
  120.1 2.4 %copy.85 = f32[32,128,128]{2,0,1:T(8,128)S(1)} copy(f32[32,128,128]{1,2,0:T(8,128)} %fusion.47) | data formatting | bytes 4194304 | tf_op jit(solution)/shard_map/scatter-add | solution.py:144
  122.5 1.9 fusion.60
  124.4 2.6 %copy.86 = f32[32,128,128]{2,1,0:T(8,128)} copy(f32[32,128,128]{2,0,1:T(8,128)S(1)} %fusion.60) | data formatting | bytes 4194304 | tf_op jit(solution)/shard_map/kz,zxy->kxy/dot_general | solution.py:38
  127.0 4.9 %all-to-all-start.1 = ((f32[32,128,128]{2,1,0:T(8,128)}), f32[32,128,128]{2,1,0:T(8,128)S(1)}, u32[]{:S(2)}, u32[]{:S(2)}) async-start(f32[32,128,128]{2,1,0:T(8,128)} %copy.86), calls=%async_computation.1 | async-start | bytes 4194304 | tf_op jit(solution)/shard_map/all_to_all | solution.py:39
  131.9 3.5 %cosine_multiply_fusion.2 = f32[512,512]{0,1:T(8,128)S(1)} fusion(f32[512]{0:T(512)S(1)} %get-tuple-element.75, f32[512]{0:T(512)S(1)} %get-tuple-element.76, f32[512]{0:T(512)S(1)} %fusion.63), kind=kLoop, calls=%fused_computation.42 | loop fusion | flops 786432 | bytes 1054720 | tf_op jit(solution)/shard_map/mul | solution.py:16
  135.5 15.1 %cosine_multiply_fusion = f32[1024,1024]{0,1:T(8,128)} fusion(f32[1024]{0:T(1024)S(1)} %get-tuple-element.73, f32[1024]{0:T(1024)S(1)} %get-tuple-element.74, f32[1024]{0:T(1024)S(1)} %fusion.62), kind=kLoop, calls=%fused_computation | loop fusion | flops 3145728 | bytes 4206592 | tf_op jit(solution)/shard_map/mul | solution.py:16
  150.5 11.3 %cosine_multiply_fusion.1 = (f32[1,512,1024]{2,1,0:T(8,128)}, f32[1,512,1024]{2,1,0:T(8,128)}) fusion(f32[1024]{0:T(1024)S(1)} %multiply_multiply_fusion.5, f32[512]{0:T(512)S(1)} %multiply_add_fusion.3), kind=kLoop, calls=%fused_computation.37 | loop fusion | flops 20447232 | bytes 4200448 | tf_op jit(solution)/shard_map/mul | solution.py:73
  161.9 0.0 all-to-all-done.1
  161.9 1.9 fusion.67
  163.8 0.3 copy-done
  164.1 7.0 %fusion.13 = f32[1,512,1024]{2,1,0:T(8,128)S(1)} fusion(f32[1,512,1024]{2,1,0:T(8,128)} %get-tuple-element.72, f32[1,1,512,1024]{3,2,1,0:T(8,128)} %param.15, f32[1,512,1024]{2,1,0:T(8,128)} %get-tuple-element.71, f32[1,1,512,1024]{3,2,1,0:T(8,128)} %param.14, f32[1024,8,128]{0,2,1:T(8,128)S(1)} %bitcast.106, f32[512,8,128,1]{2,0,1,3:T(8,128)S(1)} %fusion.67), kind=kOutput, calls=%fused_computation.22 | convolution fusion | flops 3223322624 | bytes 16777216 | tf_op jit(solution)/shard_map/cjy,bjy->bc/dot_general | solution.py:44
  171.1 0.0 copy-start.1
  171.1 3.5 %fusion.11 = f32[512,8,128]{0,2,1:T(8,128)S(1)} fusion(f32[1024,8,128]{0,2,1:T(8,128)S(1)} %bitcast.107, f32[1,512,1024]{2,1,0:T(8,128)S(1)} %fusion.13), kind=kOutput, calls=%fused_computation.19 | convolution fusion | flops 3221225472 | bytes 8388608 | tf_op jit(solution)/shard_map/cjy,bc->bjy/dot_general | solution.py:54
  174.7 0.0 copy-done.1
  174.7 1.8 fusion.24
  176.5 1.8 copy.93
  178.3 35.6 %all_to_all.22 = f32[32,128,128]{2,1,0:T(8,128)S(1)} all-to-all(f32[32,128,128]{2,1,0:T(8,128)} %bitcast.112), channel_id=1, replica_groups=mesh['grp'=4,'gx'=4,'gy'=8] {'gx','gy'}, dimensions={0} | all-to-all | bytes 4194304 | tf_op jit(solution)/shard_map/all_to_all | solution.py:57
  214.0 3.0 %fusion.21 = f32[1,32,128,128]{3,1,2,0:T(8,128)S(1)} fusion(f32[32,128,128]{2,1,0:T(8,128)S(1)} %all_to_all.22, f32[32,32]{0,1:T(8,128)S(1)} %cosine_multiply_fusion.3), kind=kOutput, calls=%fused_computation.39 | convolution fusion | flops 201326592 | bytes 4198400 | tf_op jit(solution)/shard_map/kz,kxy->zxy/dot_general | solution.py:58
  217.0 2.5 %copy.95 = f32[1,32,128,128]{3,2,1,0:T(8,128)} copy(f32[1,32,128,128]{3,1,2,0:T(8,128)S(1)} %fusion.21) | data formatting | bytes 4194304
  (20 shorter events, 0.2 us)
Async XLA Ops:
  7.2 3.8 %copy-start.4 = (s32[1,128,1]{1,2,0:T(1,128)S(1)}, s32[1,128,1]{1,2,0:T(1,128)}, u32[]{:S(2)}) copy-start(s32[1,128,1]{1,2,0:T(1,128)} %param.18) | copy-start | bytes 1540
  7.2 77.7 %all-gather.2.cloned.1.call-start = ((), (), s32[]{:S(2)}) async-start(), calls=%async_computation.3 | async-start | bytes 8454144 | tf_op jit(solution)/shard_map/all_gather | solution.py:120
  89.3 0.5 copy-start.2
  91.6 21.7 %all-to-all-start = ((f32[128,2,768]{2,1,0:T(2,128)}), f32[128,2,768]{2,1,0:T(2,128)S(1)}, u32[]{:S(2)}, u32[]{:S(2)}) async-start(f32[128,2,768]{2,1,0:T(2,128)} %all_to_all.14), calls=%async_computation | async-start | bytes 1572864 | tf_op jit(solution)/shard_map/all_to_all | solution.py:131
  101.3 14.6 %copy-start.5 = (s32[1,128,1]{1,2,0:T(1,128)S(1)}, s32[1,128,1]{1,2,0:T(1,128)}, u32[]{:S(2)}) copy-start(s32[1,128,1]{1,2,0:T(1,128)} %param.18) | copy-start | bytes 1540
  114.8 2.7 %copy-start.3 = (s32[256]{0:T(256)S(1)}, s32[256]{0:T(256)}, u32[]{:S(2)}) copy-start(s32[256]{0:T(256)} %copy-done.2) | copy-start | bytes 3076
  114.8 2.7 %copy-start.6 = (f32[256]{0:T(256)S(1)}, f32[256]{0:T(256)}, u32[]{:S(2)}) copy-start(f32[256]{0:T(256)} %reshape.636) | copy-start | bytes 3076
  127.0 34.9 %all-to-all-start.1 = ((f32[32,128,128]{2,1,0:T(8,128)}), f32[32,128,128]{2,1,0:T(8,128)S(1)}, u32[]{:S(2)}, u32[]{:S(2)}) async-start(f32[32,128,128]{2,1,0:T(8,128)} %copy.86), calls=%async_computation.1 | async-start | bytes 4194304 | tf_op jit(solution)/shard_map/all_to_all | solution.py:39
  161.9 2.2 copy-start
  171.1 3.6 %copy-start.1 = (f32[1,512,1024]{2,1,0:T(8,128)}, f32[1,512,1024]{2,1,0:T(8,128)S(1)}, u32[]{:S(2)}) copy-start(f32[1,512,1024]{2,1,0:T(8,128)S(1)} %fusion.13) | copy-start | bytes 6291460
Sparse Core Ops, SparseCore 0:
  11.5 73.2 all-gather.1
